TPU v7x, 256 devices: a whole 4x4x8 slice. The times are simulated.
256 devices in a mesh: dp: 4 (over x), expert: 64 (over y, z, core).
Axes of the slice: x: 4, y: 4, z: 8, core: 2. Of those that a mesh axis runs over, the one named last changes fastest.
Arguments:
- tokens: bfloat16 [32768, 2048], P(('dp', 'expert')), may hold values from -6 to 6
- expert_ids: int32 [32768, 8], P(('dp', 'expert')), may hold values from 0 to 63, all different within a row; in each aligned block of 128 rows (0 to 127, 128 to 255, ...) at most 24 rows name the same one
- gate_probs: float32 [32768, 8], P(('dp', 'expert')), may hold values from 0.02 to 1
- placement: int32 [64], replicated, may hold values from 0 to 63, each once
- w_gate_up: bfloat16 [64, 2, 768, 2048], P('expert', None, 'dp'), may hold values from -0.125 to 0.125
- w_down: bfloat16 [64, 768, 2048], P('expert', 'dp'), may hold values from -0.21875 to 0.21875
Outputs:
- critic_mix: bfloat16 [32768, 2048], P(('dp', 'expert'))
- placed_gate_up: bfloat16 [64, 2, 768, 2048], P('expert', None, 'dp')
- placed_down: bfloat16 [64, 768, 2048], P('expert', 'dp')
Inputs may be any that keep to these rules, and one draw needn't show every extreme that they name: `expert_ids`: each token names 8 different experts; among the 128 tokens of one device at most 24 name the same expert, and some device reaches 24. `placement`: A permutation of the expert numbers.
All inputs are finite; a program needn't handle non-finite values.
Results may differ from a plain program's by a relative error of at most 0.0058.
Values may be sent and summed in bfloat16 or wider, within the bound.
No kernel may reach another device: no remote copies, remote signals or barrier semaphores. Data moves between devices by JAX's collectives and lax.ppermute only.
A program may use at most 128 MiB of HBM per device.

v0:
```python
import jax
import jax.numpy as jnp
from jax import lax
from jax.sharding import PartitionSpec as P


def per_device(tokens, expert_ids, gate_probs, placement, w_gate_up, w_down):
    tok_dev = tokens.shape[0]
    model_width = tokens.shape[1]
    top_count = expert_ids.shape[1]
    experts = placement.shape[0]
    capacity = min(tok_dev, 3 * tok_dev * top_count // (2 * experts))
    numbers = jnp.arange(experts, dtype=jnp.int32)
    inverse = jnp.sum(
        jnp.where(placement[:, None] == numbers[None, :], numbers[:, None], 0), axis=0
    )
    flat_ids = expert_ids.reshape(-1)
    onehot = (flat_ids[:, None] == numbers[None, :]).astype(jnp.int32)
    before = jnp.cumsum(onehot, axis=0) - onehot
    slot_of = jnp.sum(before * onehot, axis=1)
    down_four = w_down.reshape((1, 1) + w_down.shape[1:])
    pieces = (
        lax.all_to_all(w_gate_up, "expert", split_axis=3, concat_axis=0, tiled=True),
        lax.all_to_all(down_four, "expert", split_axis=3, concat_axis=0, tiled=True),
    )
    reordered = (jnp.take(pieces[0], inverse, axis=0), jnp.take(pieces[1], inverse, axis=0))
    placed = (
        lax.all_to_all(reordered[0], "expert", split_axis=0, concat_axis=3, tiled=True),
        lax.all_to_all(reordered[1], "expert", split_axis=0, concat_axis=3, tiled=True),
    )
    placed_gate_up = placed[0]
    placed_down = placed[1].reshape(w_down.shape)
    gathered = (
        lax.all_gather(placed[0], "dp", axis=2, tiled=True),
        lax.all_gather(placed[1], "dp", axis=2, tiled=True),
    )
    hidden_count = gathered[0].shape[2]
    gate_up_full = gathered[0].reshape(2 * hidden_count, model_width)
    down_full = gathered[1].reshape(hidden_count, model_width)
    flat_index = flat_ids * capacity + slot_of
    spread_rows = jnp.broadcast_to(tokens[:, None, :], (tok_dev, top_count, model_width)).reshape(
        -1, model_width
    )
    buffer = (
        jnp.zeros((experts * capacity, model_width), jnp.bfloat16).at[flat_index].set(spread_rows)
    )
    buffer = buffer.reshape(experts, capacity, model_width)
    received = lax.all_to_all(buffer, "expert", split_axis=0, concat_axis=0, tiled=True)
    row_block = received.reshape(-1, model_width)
    projected = lax.dot_general(
        row_block, gate_up_full, (((1,), (1,)), ((), ())), preferred_element_type=jnp.float32
    )
    gate_part = projected[:, :hidden_count]
    up_part = projected[:, hidden_count:]
    hidden = (jax.nn.silu(gate_part) * up_part).astype(jnp.bfloat16)
    result = jnp.dot(hidden, down_full, preferred_element_type=jnp.float32).astype(jnp.bfloat16)
    result = result.reshape(received.shape)
    returned = lax.all_to_all(result, "expert", split_axis=0, concat_axis=0, tiled=True)
    flat_out = returned.reshape(experts * capacity, model_width)
    picked = flat_out[flat_index].reshape(tok_dev, top_count, model_width)
    gates = gate_probs / jnp.sum(gate_probs, axis=1, keepdims=True)
    mixed_rows = jnp.einsum(
        "tk,tkd->td",
        gates,
        picked,
        preferred_element_type=jnp.float32,
        precision=lax.Precision.HIGHEST,
    )
    return (mixed_rows.astype(jnp.bfloat16), placed_gate_up, placed_down)


def solution(mesh):
    in_specs = (
        P(("dp", "expert"), None),
        P(("dp", "expert"), None),
        P(("dp", "expert"), None),
        P(),
        P("expert", None, "dp", None),
        P("expert", "dp", None),
    )
    out_specs = (P(("dp", "expert"), None), P("expert", None, "dp", None), P("expert", "dp", None))
    return jax.shard_map(
        per_device, mesh=mesh, in_specs=in_specs, out_specs=out_specs, check_vma=False
    )
```

profile of v0, /device:TPU:1, one launch (start us, length us, event | category | flops | bytes accessed | tf_op | source)
XLA Modules:
  0.0 561.2 jit_solution(7574284037175607885)
XLA Ops:
  7.2 0.0 copy-start
  7.2 4.6 copy.75
  11.8 0.5 broadcast.106
  12.3 12.6 %reduce = bf16[2048,192]{1,0:T(8,128)(2,1)} reduce(bf16[2048,1,1,192]{3,2,1,0:T(2,128)(2,1)S(1)} %bitcast.83, bf16[]{:T(256)} %broadcast.106), dimensions={1,2}, to_apply=%bitcast.70.reduce_sub_computation | reduce | bytes 1572866
  24.9 3.7 reshape.162
  28.6 13.2 %all-to-all-start.3 = ((bf16[64,2,3072]{2,1,0:T(2,128)(2,1)}), bf16[64,2,3072]{2,1,0:T(2,128)(2,1)S(1)}, u32[]{:S(2)}, u32[]{:S(2)}) async-start(bf16[64,2,3072]{2,1,0:T(2,128)(2,1)} %reshape.162), calls=%async_computation.3 | async-start | bytes 1572864 | tf_op jit(solution)/shard_map/all_to_all | solution.py:24
  41.7 0.0 copy-done.3
  41.7 0.0 copy-start.6
  41.8 3.8 copy.69
  45.5 19.2 %all-to-all-done.3 = bf16[64,2,3072]{2,1,0:T(2,128)(2,1)S(1)} async-done(((bf16[64,2,3072]{2,1,0:T(2,128)(2,1)}), bf16[64,2,3072]{2,1,0:T(2,128)(2,1)S(1)}, u32[]{:S(2)}, u32[]{:S(2)}) %all-to-all-start.3) | async-done | bytes 786464 | tf_op jit(solution)/shard_map/all_to_all | solution.py:24
  64.7 6.4 %all-to-all-start.1 = ((bf16[1,2,192,2048]{2,1,0,3:T(2,128)(2,1)}), bf16[1,2,192,2048]{2,1,0,3:T(2,128)(2,1)}, u32[]{:S(2)}, u32[]{:S(2)}) async-start(bf16[1,2,192,2048]{2,1,0,3:T(2,128)(2,1)} %copy.69), calls=%async_computation.1 | async-start | bytes 4194304 | tf_op jit(solution)/shard_map/all_to_all | solution.py:23
  71.1 0.0 copy-done.6
  71.1 0.1 select_reduce_fusion
  71.2 3.7 reshape.163
  75.0 1.8 copy.84
  76.7 0.6 gather_fusion.1
  77.4 1.1 fusion.10
  78.5 43.8 %all-to-all-done.1 = bf16[1,2,192,2048]{2,1,0,3:T(2,128)(2,1)} async-done(((bf16[1,2,192,2048]{2,1,0,3:T(2,128)(2,1)}), bf16[1,2,192,2048]{2,1,0,3:T(2,128)(2,1)}, u32[]{:S(2)}, u32[]{:S(2)}) %all-to-all-start.1) | async-done | bytes 1572896 | tf_op jit(solution)/shard_map/all_to_all | solution.py:23
  122.3 6.0 %all-to-all-start.4 = ((bf16[64,1,192,32]{2,3,1,0:T(8,128)(2,1)}), bf16[64,1,192,32]{2,3,1,0:T(8,128)(2,1)}, u32[]{:S(2)}, u32[]{:S(2)}) async-start(bf16[64,1,192,32]{2,3,1,0:T(8,128)(2,1)} %fusion.10), calls=%async_computation.4 | async-start | bytes 2097152 | tf_op jit(solution)/shard_map/all_to_all | solution.py:29
  128.3 3.4 copy.89
  131.7 2.3 gather_fusion
  133.9 0.0 copy-start.4
  133.9 1.6 broadcast_select_fusion
  135.6 21.2 %all-to-all-done.4 = bf16[64,1,192,32]{2,3,1,0:T(8,128)(2,1)} async-done(((bf16[64,1,192,32]{2,3,1,0:T(8,128)(2,1)}), bf16[64,1,192,32]{2,3,1,0:T(8,128)(2,1)}, u32[]{:S(2)}, u32[]{:S(2)}) %all-to-all-start.4) | async-done | bytes 786464 | tf_op jit(solution)/shard_map/all_to_all | solution.py:29
  156.8 6.2 %all-to-all-start.2 = ((bf16[64,2,192,32]{2,3,1,0:T(8,128)(2,1)}), bf16[64,2,192,32]{2,3,1,0:T(8,128)(2,1)S(1)}, u32[]{:S(2)}, u32[]{:S(2)}) async-start(bf16[64,2,192,32]{2,3,1,0:T(8,128)(2,1)} %broadcast_select_fusion), calls=%async_computation.2 | async-start | bytes 4194304 | tf_op jit(solution)/shard_map/all_to_all | solution.py:28
  163.0 0.0 copy-done.4
  163.0 0.1 copy.65
  163.1 0.1 eq.42
  163.2 0.1 eq.38
  163.3 18.0 %reduce-window.6 = s32[64,8,128]{2,1,0:T(8,128)S(1)} reduce-window(s32[64,8,128]{2,1,0:T(8,128)S(1)} %fusion.14, s32[]{:T(128)} %constant.32.clone.1), window={size=1x1x128 pad=0_0x0_0x127_0}, to_apply=%region_1.2 | reduce-window | flops 8323072 | bytes 524292 | tf_op jit(solution)/shard_map/reduce-window
  181.3 0.1 slice.22
  181.4 0.1 copy.67
  181.6 0.1 copy.68
  181.7 0.1 copy.64
  181.8 0.1 mul.28
  181.9 0.1 broadcast_add_fusion
  182.1 0.1 fusion.13
  182.2 0.0 copy-done
  182.2 10.2 %scatter_custom_fusion = bf16[1536,2048]{1,0:T(8,128)(2,1)} fusion(s32[1024]{0:T(1024)S(1)} %bitcast.92, bf16[]{:T(256)} %constant.24.clone.1, bf16[128,2048]{1,0:T(8,128)(2,1)S(1)} %copy-done), kind=kCustom, calls=%fused_computation.9 | custom fusion | bytes 6815746 | tf_op jit(solution)/shard_map/scatter | solution.py:45
  192.4 21.8 %all-to-all-done.2 = bf16[64,2,192,32]{2,3,1,0:T(8,128)(2,1)S(1)} async-done(((bf16[64,2,192,32]{2,3,1,0:T(8,128)(2,1)}), bf16[64,2,192,32]{2,3,1,0:T(8,128)(2,1)S(1)}, u32[]{:S(2)}, u32[]{:S(2)}) %all-to-all-start.2) | async-done | bytes 1572896 | tf_op jit(solution)/shard_map/all_to_all | solution.py:28
  214.2 6.0 %all-to-all-start = ((bf16[64,24,2048]{2,1,0:T(8,128)(2,1)}), bf16[64,24,2048]{2,1,0:T(8,128)(2,1)}, u32[]{:S(2)}, u32[]{:S(2)}) async-start(bf16[64,24,2048]{2,1,0:T(8,128)(2,1)} %bitcast.78), calls=%async_computation | async-start | bytes 12582912 | tf_op jit(solution)/shard_map/all_to_all | solution.py:48
  220.2 0.0 all-gather.3.cloned.1.call-start
  220.2 0.0 copy-done.2
  220.3 1.8 copy.72
  222.1 3.3 copy.73
  225.4 0.0 all-gather.3.cloned.1.call-update
  225.4 0.3 all-gather.5.cloned.1.call-start
  225.7 2.2 copy.77
  227.9 0.0 all-gather.5.cloned.1.call-update
  227.9 66.8 %all-gather.3.cloned.1.call-done = bf16[1,2,768,2048]{3,1,0,2:T(2,128)(2,1)} async-done(((bf16[1,2,192,2048]{3,1,0,2:T(2,128)(2,1)}), bf16[1,2,768,2048]{3,1,0,2:T(2,128)(2,1)}) %all-gather.3.cloned.1.call-update) | async-done | bytes 6291472 | tf_op jit(solution)/shard_map/all_gather | solution.py:34
  294.7 8.3 %copy.74 = bf16[1,2,768,2048]{3,2,1,0:T(8,128)(2,1)} copy(bf16[1,2,768,2048]{3,1,0,2:T(2,128)(2,1)} %all-gather.3.cloned.1.call-done) | data formatting | bytes 12582912 | tf_op jit(solution)/shard_map/all_gather | solution.py:34
  303.0 58.0 %all-to-all-done = bf16[64,24,2048]{2,1,0:T(8,128)(2,1)} async-done(((bf16[64,24,2048]{2,1,0:T(8,128)(2,1)}), bf16[64,24,2048]{2,1,0:T(8,128)(2,1)}, u32[]{:S(2)}, u32[]{:S(2)}) %all-to-all-start) | async-done | bytes 6291488 | tf_op jit(solution)/shard_map/all_to_all | solution.py:48
  361.0 15.7 %fusion.17 = f32[1536,1536]{1,0:T(8,128)} fusion(bf16[1536,2048]{1,0:T(8,128)(2,1)} %bitcast.7, bf16[1536,2048]{1,0:T(8,128)(2,1)} %bitcast.86), kind=kOutput, calls=%fused_computation.40 | convolution fusion | flops 9663676416 | bytes 22020096 | tf_op jit(solution)/shard_map/dot_general | solution.py:50
  376.8 11.4 %convolution_convert_fusion = bf16[1536,2048]{1,0:T(8,128)(2,1)} fusion(bf16[1,1,768,2048]{3,2,1,0:T(8,128)(2,1)} %all-gather.5.cloned.1.call-done, f32[1536,1536]{1,0:T(8,128)} %fusion.17), kind=kOutput, calls=%fused_computation.4 | convolution fusion | flops 4842061824 | bytes 18874368 | tf_op jit(solution)/shard_map/dot_general | solution.py:56
  388.1 6.1 %all-to-all-start.5 = ((bf16[64,24,2048]{2,1,0:T(8,128)(2,1)}), bf16[64,24,2048]{2,1,0:T(8,128)(2,1)}, u32[]{:S(2)}, u32[]{:S(2)}) async-start(bf16[64,24,2048]{2,1,0:T(8,128)(2,1)} %bitcast.85), calls=%async_computation.5 | async-start | bytes 12582912 | tf_op jit(solution)/shard_map/all_to_all | solution.py:58
  394.2 0.0 copy-done.5
  394.3 0.1 copy.80
  394.4 2.2 copy.79
  396.6 2.2 copy.78
  398.8 136.3 %all-to-all-done.5 = bf16[64,24,2048]{2,1,0:T(8,128)(2,1)} async-done(((bf16[64,24,2048]{2,1,0:T(8,128)(2,1)}), bf16[64,24,2048]{2,1,0:T(8,128)(2,1)}, u32[]{:S(2)}, u32[]{:S(2)}) %all-to-all-start.5) | async-done | bytes 6291488 | tf_op jit(solution)/shard_map/all_to_all | solution.py:58
  535.1 12.4 %gather_fusion.2 = bf16[1024,2048]{1,0:T(8,128)(2,1)} fusion(bf16[1536,2048]{1,0:T(8,128)(2,1)} %bitcast.27, s32[1024]{0:T(1024)S(1)} %broadcast_clamp_fusion), kind=kCustom, calls=%fused_computation.2 | custom fusion | bytes 8392704 | tf_op jit(solution)/shard_map/gather | solution.py:60
  547.5 5.7 %fusion.1 = bf16[128,1,2048]{2,1,0:T(2,128)(2,1)S(1)} fusion(f32[128,8,1]{1,2,0:T(1,128)S(1)} %copy.80, bf16[1024,2048]{1,0:T(8,128)(2,1)} %gather_fusion.2), kind=kOutput, calls=%fused_computation.7 | convolution fusion | flops 25165824 | bytes 4722688 | tf_op jit(solution)/shard_map/tk,tkd->td/dot_general | solution.py:62
  553.3 1.1 copy.90
  554.3 0.0 copy-done.1
  (16 shorter events, 0.1 us)
Async XLA Ops:
  7.2 175.0 %copy-start = (bf16[128,2048]{1,0:T(8,128)(2,1)S(1)}, bf16[128,2048]{1,0:T(8,128)(2,1)}, u32[]{:S(2)}) copy-start(bf16[128,2048]{1,0:T(8,128)(2,1)} %param.6) | copy-start | bytes 1572868
  24.9 16.8 %copy-start.3 = (bf16[1,2,192,2048]{3,2,1,0:T(8,128)(2,1)S(1)}, bf16[1,2,192,2048]{3,2,1,0:T(8,128)(2,1)}, u32[]{:S(2)}) copy-start(bf16[1,2,192,2048]{3,2,1,0:T(8,128)(2,1)} %param.10) | copy-start | bytes 4718596
  28.6 36.1 %all-to-all-start.3 = ((bf16[64,2,3072]{2,1,0:T(2,128)(2,1)}), bf16[64,2,3072]{2,1,0:T(2,128)(2,1)S(1)}, u32[]{:S(2)}, u32[]{:S(2)}) async-start(bf16[64,2,3072]{2,1,0:T(2,128)(2,1)} %reshape.162), calls=%async_computation.3 | async-start | bytes 1572864 | tf_op jit(solution)/shard_map/all_to_all | solution.py:24
  41.7 29.4 %copy-start.6 = (s32[64]{0:T(128)S(1)}, s32[64]{0:T(128)}, u32[]{:S(2)}) copy-start(s32[64]{0:T(128)} %param.9) | copy-start | bytes 772
  64.7 57.6 %all-to-all-start.1 = ((bf16[1,2,192,2048]{2,1,0,3:T(2,128)(2,1)}), bf16[1,2,192,2048]{2,1,0,3:T(2,128)(2,1)}, u32[]{:S(2)}, u32[]{:S(2)}) async-start(bf16[1,2,192,2048]{2,1,0,3:T(2,128)(2,1)} %copy.69), calls=%async_computation.1 | async-start | bytes 4194304 | tf_op jit(solution)/shard_map/all_to_all | solution.py:23
  122.3 34.5 %all-to-all-start.4 = ((bf16[64,1,192,32]{2,3,1,0:T(8,128)(2,1)}), bf16[64,1,192,32]{2,3,1,0:T(8,128)(2,1)}, u32[]{:S(2)}, u32[]{:S(2)}) async-start(bf16[64,1,192,32]{2,3,1,0:T(8,128)(2,1)} %fusion.10), calls=%async_computation.4 | async-start | bytes 2097152 | tf_op jit(solution)/shard_map/all_to_all | solution.py:29
  133.9 29.0 %copy-start.4 = (s32[128,8]{0,1:T(8,128)S(1)}, s32[128,8]{0,1:T(8,128)}, u32[]{:S(2)}) copy-start(s32[128,8]{0,1:T(8,128)} %param.7) | copy-start | bytes 12292
  156.8 57.4 %all-to-all-start.2 = ((bf16[64,2,192,32]{2,3,1,0:T(8,128)(2,1)}), bf16[64,2,192,32]{2,3,1,0:T(8,128)(2,1)S(1)}, u32[]{:S(2)}, u32[]{:S(2)}) async-start(bf16[64,2,192,32]{2,3,1,0:T(8,128)(2,1)} %broadcast_select_fusion), calls=%async_computation.2 | async-start | bytes 4194304 | tf_op jit(solution)/shard_map/all_to_all | solution.py:28
  214.2 6.0 %copy-start.2 = (bf16[64,2,192,32]{2,3,1,0:T(8,128)(2,1)}, bf16[64,2,192,32]{2,3,1,0:T(8,128)(2,1)S(1)}, u32[]{:S(2)}) copy-start(bf16[64,2,192,32]{2,3,1,0:T(8,128)(2,1)S(1)} %all-to-all-done.2) | copy-start | bytes 4718596
  214.2 146.8 %all-to-all-start = ((bf16[64,24,2048]{2,1,0:T(8,128)(2,1)}), bf16[64,24,2048]{2,1,0:T(8,128)(2,1)}, u32[]{:S(2)}, u32[]{:S(2)}) async-start(bf16[64,24,2048]{2,1,0:T(8,128)(2,1)} %bitcast.78), calls=%async_computation | async-start | bytes 12582912 | tf_op jit(solution)/shard_map/all_to_all | solution.py:48
  220.2 74.5 %all-gather.3.cloned.1.call-start = ((), (), s32[]{:S(2)}) async-start(), calls=%async_computation.6 | async-start | bytes 7864320 | tf_op jit(solution)/shard_map/all_gather | solution.py:34
  225.4 151.3 %all-gather.5.cloned.1.call-start = ((), (), s32[]{:S(2)}) async-start(), calls=%async_computation.7 | async-start | bytes 3932160 | tf_op jit(solution)/shard_map/all_gather | solution.py:35
  388.1 6.1 %copy-start.5 = (f32[128,8]{0,1:T(8,128)S(1)}, f32[128,8]{0,1:T(8,128)}, u32[]{:S(2)}) copy-start(f32[128,8]{0,1:T(8,128)} %param.8) | copy-start | bytes 12292
  388.1 146.9 %all-to-all-start.5 = ((bf16[64,24,2048]{2,1,0:T(8,128)(2,1)}), bf16[64,24,2048]{2,1,0:T(8,128)(2,1)}, u32[]{:S(2)}, u32[]{:S(2)}) async-start(bf16[64,24,2048]{2,1,0:T(8,128)(2,1)} %bitcast.85), calls=%async_computation.5 | async-start | bytes 12582912 | tf_op jit(solution)/shard_map/all_to_all | solution.py:58
  535.1 19.3 %copy-start.1 = (bf16[128,2048]{1,0:T(8,128)(2,1)S(1)}, bf16[128,2048]{1,0:T(8,128)(2,1)}, u32[]{:S(2)}) copy-start(bf16[128,2048]{1,0:T(8,128)(2,1)} %param.6) | copy-start | bytes 1572868
Sparse Core Ops, SparseCore 0:
  225.5 69.1 all-gather.2
  297.1 42.7 all-gather.4
where the time goes:
time: 562 us; the launch traced here: 561 us
  waiting for transfers between devices  367 us (65%)
  local copies, waits for them, and re-layouts  69.1 us (12%)
  starting transfers between devices  44.1 us (8%)
  other arithmetic  33.8 us (6%)
  matrix products  32.8 us (6%)
  between operations  14.3 us (3%)
    all_to_all x1, waiting for transfers between devices, per_device(): lax.all_to_all(result, 'expert', split_axis=0, concat_axis=0, tiled=True)  136 us
    all_gather x1, waiting for transfers between devices, per_device(): lax.all_gather(placed[0], 'dp', axis=2, tiled=True)  66.8 us
    all_to_all x1, waiting for transfers between devices, per_device(): lax.all_to_all(buffer, 'expert', split_axis=0, concat_axis=0, tiled=True)  58 us
    all_to_all x1, waiting for transfers between devices, per_device(): lax.all_to_all(w_gate_up, 'expert', split_axis=3, concat_axis=0, tiled=True)  43.8 us
    all_to_all x1, waiting for transfers between devices, per_device(): lax.all_to_all(reordered[0], 'expert', split_axis=0, concat_axis=3, tiled...  21.8 us
    all_to_all x1, waiting for transfers between devices, per_device(): lax.all_to_all(reordered[1], 'expert', split_axis=0, concat_axis=3, tiled...  21.2 us
    all_to_all x1, waiting for transfers between devices, per_device(): lax.all_to_all(down_four, 'expert', split_axis=3, concat_axis=0, tiled=True)  19.2 us
    another operation x3, other arithmetic  18.2 us
  transfers between devices with their start and end apart: 8, of which 7 were waited for; matrix products, arithmetic and copies ran while one was open for 15% of the time, Pallas kernels for 0%

commit v1 on v0

--- a/solution.py
+++ b/solution.py
@@ -2,6 +2,14 @@
 import jax.numpy as jnp
 from jax import lax
 from jax.sharding import PartitionSpec as P
+
+
+def gather_from_all(value, axis, dim):
+    size = lax.axis_size(axis)
+    repeats = [size if d == dim else 1 for d in range(value.ndim)]
+    return lax.all_to_all(
+        jnp.tile(value, repeats), axis, split_axis=dim, concat_axis=dim, tiled=True
+    )
 
 
 def per_device(tokens, expert_ids, gate_probs, placement, w_gate_up, w_down):
@@ -31,7 +39,7 @@
     placed_gate_up = placed[0]
     placed_down = placed[1].reshape(w_down.shape)
     gathered = (
-        lax.all_gather(placed[0], "dp", axis=2, tiled=True),
+        gather_from_all(placed[0], "dp", 2),
         lax.all_gather(placed[1], "dp", axis=2, tiled=True),
     )
     hidden_count = gathered[0].shape[2]

time: 562 us -> 630 us (1.12)
  waiting for transfers between devices: 367 us -> 421 us
    all_to_all x1, waiting for transfers between devices: 58 us -> 130 us  [per_device(): lax.all_to_all(buffer, 'expert', split_axis=0, concat_axis=0, tiled=True)]
    all_gather x1 -> x0, waiting for transfers between devices: 66.8 us -> none  [per_device(): lax.all_gather(placed[0], 'dp', axis=2, tiled=True)]
    all_to_all x0 -> x1, waiting for transfers between devices: none -> 41.9 us  [gather_from_all(): lax.all_to_all(jnp.tile(value, repeats), axis, split_axis=dim, concat_axi...]
    all_to_all x1, waiting for transfers between devices: 21.8 us -> 43.9 us  [per_device(): lax.all_to_all(reordered[0], 'expert', split_axis=0, concat_axis=3, tiled...]
    all_to_all x1, waiting for transfers between devices: 43.8 us -> 29.8 us  [per_device(): lax.all_to_all(w_gate_up, 'expert', split_axis=3, concat_axis=0, tiled=True)]
    another operation x2 -> x4, local copies, waits for them, and re-layouts: 0.09 us -> 9.33 us  [the longest x2 9.25 us: gather_from_all(): jnp.tile(value, repeats)]
    all_to_all x0 -> x1, local copies, waits for them, and re-layouts: none -> 8.33 us  [gather_from_all(): lax.all_to_all(jnp.tile(value, repeats), axis, split_axis=dim, concat_axi...]
    all_gather x1 -> x0, local copies, waits for them, and re-layouts: 8.29 us -> none  [per_device(): lax.all_gather(placed[0], 'dp', axis=2, tiled=True)]
  transfers between devices with their start and end apart: 8 -> 8, of which waited for: 7 -> 7; matrix products, arithmetic and copies ran while one was open for 15% -> 16% of each run, Pallas kernels for 0% -> 0%
where the time goes in v1:
time: 630 us; the launch traced here: 629 us
  waiting for transfers between devices  421 us (67%)
  local copies, waits for them, and re-layouts  74.9 us (12%)
  starting transfers between devices  49.9 us (8%)
  other arithmetic  36.4 us (6%)
  matrix products  32.7 us (5%)
  between operations  14.3 us (2%)
    all_to_all x1, waiting for transfers between devices, per_device(): lax.all_to_all(result, 'expert', split_axis=0, concat_axis=0, tiled=True)  136 us
    all_to_all x1, waiting for transfers between devices, per_device(): lax.all_to_all(buffer, 'expert', split_axis=0, concat_axis=0, tiled=True)  130 us
    all_to_all x1, waiting for transfers between devices, per_device(): lax.all_to_all(reordered[0], 'expert', split_axis=0, concat_axis=3, tiled...  43.9 us
    all_to_all x1, waiting for transfers between devices, gather_from_all(): lax.all_to_all(jnp.tile(value, repeats), axis, split_axis=dim, concat_axi...  41.9 us
    all_to_all x1, waiting for transfers between devices, per_device(): lax.all_to_all(w_gate_up, 'expert', split_axis=3, concat_axis=0, tiled=True)  29.8 us
    all_to_all x1, waiting for transfers between devices, per_device(): lax.all_to_all(reordered[1], 'expert', split_axis=0, concat_axis=3, tiled...  23.3 us
    unnamed x22, local copies, waits for them, and re-layouts  20.3 us
    another operation x3, other arithmetic  18.2 us
  transfers between devices with their start and end apart: 8, of which 7 were waited for; matrix products, arithmetic and copies ran while one was open for 16% of the time, Pallas kernels for 0%

profile of v1, /device:TPU:1, one launch (start us, length us, event | category | flops | bytes accessed | tf_op | source)
XLA Modules:
  0.0 628.8 jit_solution(14701997997527123295)
XLA Ops:
  7.2 0.0 copy-start
  7.2 0.0 copy-start.3
  7.2 6.1 copy.60
  13.3 13.2 %all-to-all-start.1 = ((bf16[1,2,192,2048]{2,1,0,3:T(2,128)(2,1)}), bf16[1,2,192,2048]{2,1,0,3:T(2,128)(2,1)S(1)}, u32[]{:S(2)}, u32[]{:S(2)}) async-start(bf16[1,2,192,2048]{2,1,0,3:T(2,128)(2,1)} %copy.60), calls=%async_computation.1 | async-start | bytes 4194304 | tf_op jit(solution)/shard_map/all_to_all | solution.py:31
  26.5 0.0 copy-done.3
  26.5 0.0 copy-start.6
  26.5 3.7 copy.66
  30.3 0.5 broadcast.109
  30.8 13.6 %reduce = bf16[2048,192]{1,0:T(8,128)(2,1)} reduce(bf16[2048,1,1,192]{3,2,1,0:T(2,128)(2,1)} %bitcast.86, bf16[]{:T(256)} %broadcast.109), dimensions={1,2}, to_apply=%bitcast.72.reduce_sub_computation | reduce | bytes 1572866
  44.4 3.5 reshape.169
  48.0 29.8 %all-to-all-done.1 = bf16[1,2,192,2048]{2,1,0,3:T(2,128)(2,1)S(1)} async-done(((bf16[1,2,192,2048]{2,1,0,3:T(2,128)(2,1)}), bf16[1,2,192,2048]{2,1,0,3:T(2,128)(2,1)S(1)}, u32[]{:S(2)}, u32[]{:S(2)}) %all-to-all-start.1) | async-done | bytes 1572896 | tf_op jit(solution)/shard_map/all_to_all | solution.py:31
  77.8 5.8 all-to-all-start.4
  83.6 0.0 copy-done.6
  83.6 0.1 select_reduce_fusion
  83.7 0.0 copy-done.2
  83.7 2.1 copy.81
  85.8 2.0 gather_fusion
  87.8 3.2 broadcast_select_fusion
  91.0 15.6 %all-to-all-done.4 = bf16[64,2,3072]{2,1,0:T(2,128)(2,1)S(1)} async-done(((bf16[64,2,3072]{2,1,0:T(2,128)(2,1)}), bf16[64,2,3072]{2,1,0:T(2,128)(2,1)S(1)}, u32[]{:S(2)}, u32[]{:S(2)}) %all-to-all-start.4) | async-done | bytes 786464 | tf_op jit(solution)/shard_map/all_to_all | solution.py:32
  106.6 6.4 %all-to-all-start.2 = ((bf16[64,2,192,32]{2,3,1,0:T(8,128)(2,1)}), bf16[64,2,192,32]{2,3,1,0:T(8,128)(2,1)}, u32[]{:S(2)}, u32[]{:S(2)}) async-start(bf16[64,2,192,32]{2,3,1,0:T(8,128)(2,1)} %broadcast_select_fusion), calls=%async_computation.2 | async-start | bytes 4194304 | tf_op jit(solution)/shard_map/all_to_all | solution.py:36
  113.0 3.8 reshape.170
  116.7 1.8 copy.76
  118.5 0.6 gather_fusion.1
  119.1 1.1 fusion.10
  120.3 43.9 %all-to-all-done.2 = bf16[64,2,192,32]{2,3,1,0:T(8,128)(2,1)} async-done(((bf16[64,2,192,32]{2,3,1,0:T(8,128)(2,1)}), bf16[64,2,192,32]{2,3,1,0:T(8,128)(2,1)}, u32[]{:S(2)}, u32[]{:S(2)}) %all-to-all-start.2) | async-done | bytes 1572896 | tf_op jit(solution)/shard_map/all_to_all | solution.py:36
  164.1 6.0 all-to-all-start.5
  170.1 1.8 copy.63
  171.9 3.3 copy.64
  175.3 23.3 %all-to-all-done.5 = bf16[64,1,192,32]{2,3,1,0:T(8,128)(2,1)} async-done(((bf16[64,1,192,32]{2,3,1,0:T(8,128)(2,1)}), bf16[64,1,192,32]{2,3,1,0:T(8,128)(2,1)}, u32[]{:S(2)}, u32[]{:S(2)}) %all-to-all-start.5) | async-done | bytes 786464 | tf_op jit(solution)/shard_map/all_to_all | solution.py:37
  198.6 5.9 tile.12
  204.5 5.5 all-to-all-start.3
  210.1 0.0 copy-done.4
  210.1 0.1 copy.56
  210.2 0.1 eq.42
  210.3 0.1 eq.38
  210.4 18.0 %reduce-window.6 = s32[64,8,128]{2,1,0:T(8,128)S(1)} reduce-window(s32[64,8,128]{2,1,0:T(8,128)S(1)} %fusion.14, s32[]{:T(128)} %constant.32.clone.1), window={size=1x1x128 pad=0_0x0_0x127_0}, to_apply=%region_1.2 | reduce-window | flops 8323072 | bytes 524292 | tf_op jit(solution)/shard_map/reduce-window
  228.4 0.1 slice.22
  228.5 0.1 copy.58
  228.7 0.1 copy.59
  228.8 0.1 copy.55
  228.9 0.1 mul.28
  229.0 0.1 broadcast_add_fusion
  229.1 0.1 fusion.13
  229.2 0.0 copy-done
  229.2 10.2 %scatter_custom_fusion = bf16[1536,2048]{1,0:T(8,128)(2,1)} fusion(s32[1024]{0:T(1024)S(1)} %bitcast.95, bf16[]{:T(256)} %constant.24.clone.1, bf16[128,2048]{1,0:T(8,128)(2,1)S(1)} %copy-done), kind=kCustom, calls=%fused_computation.9 | custom fusion | bytes 6815746 | tf_op jit(solution)/shard_map/scatter | solution.py:53
  239.4 41.9 %all-to-all-done.3 = bf16[1,2,768,2048]{3,1,0,2:T(2,128)(2,1)} async-done(((bf16[1,2,768,2048]{3,1,0,2:T(2,128)(2,1)}), bf16[1,2,768,2048]{3,1,0,2:T(2,128)(2,1)}, u32[]{:S(2)}, u32[]{:S(2)}) %all-to-all-start.3) | async-done | bytes 6291488 | tf_op jit(solution)/shard_map/all_to_all | solution.py:10
  281.3 6.6 %all-to-all-start = ((bf16[64,24,2048]{2,1,0:T(8,128)(2,1)}), bf16[64,24,2048]{2,1,0:T(8,128)(2,1)}, u32[]{:S(2)}, u32[]{:S(2)}) async-start(bf16[64,24,2048]{2,1,0:T(8,128)(2,1)} %bitcast.80), calls=%async_computation | async-start | bytes 12582912 | tf_op jit(solution)/shard_map/all_to_all | solution.py:56
  288.0 0.3 all-gather.2.cloned.1.call-start
  288.2 2.2 copy.68
  290.4 0.0 all-gather.2.cloned.1.call-update
  290.4 8.3 %copy.65 = bf16[1,2,768,2048]{3,2,1,0:T(8,128)(2,1)} copy(bf16[1,2,768,2048]{3,1,0,2:T(2,128)(2,1)} %all-to-all-done.3) | data formatting | bytes 12582912 | tf_op jit(solution)/shard_map/all_to_all | solution.py:10
  298.8 130.0 %all-to-all-done = bf16[64,24,2048]{2,1,0:T(8,128)(2,1)} async-done(((bf16[64,24,2048]{2,1,0:T(8,128)(2,1)}), bf16[64,24,2048]{2,1,0:T(8,128)(2,1)}, u32[]{:S(2)}, u32[]{:S(2)}) %all-to-all-start) | async-done | bytes 6291488 | tf_op jit(solution)/shard_map/all_to_all | solution.py:56
  428.8 15.6 %fusion.17 = f32[1536,1536]{1,0:T(8,128)} fusion(bf16[1536,2048]{1,0:T(8,128)(2,1)} %bitcast.7, bf16[1536,2048]{1,0:T(8,128)(2,1)} %bitcast.89), kind=kOutput, calls=%fused_computation.40 | convolution fusion | flops 9663676416 | bytes 22020096 | tf_op jit(solution)/shard_map/dot_general | solution.py:58
  444.4 11.4 %convolution_convert_fusion = bf16[1536,2048]{1,0:T(8,128)(2,1)} fusion(bf16[1,1,768,2048]{3,2,1,0:T(8,128)(2,1)} %all-gather.2.cloned.1.call-done, f32[1536,1536]{1,0:T(8,128)} %fusion.17), kind=kOutput, calls=%fused_computation.4 | convolution fusion | flops 4842061824 | bytes 18874368 | tf_op jit(solution)/shard_map/dot_general | solution.py:64
  455.8 6.1 all-to-all-start.6
  461.9 0.0 copy-done.5
  461.9 0.1 copy.72
  462.0 2.2 copy.71
  464.2 2.2 copy.70
  466.4 136.3 %all-to-all-done.6 = bf16[64,24,2048]{2,1,0:T(8,128)(2,1)} async-done(((bf16[64,24,2048]{2,1,0:T(8,128)(2,1)}), bf16[64,24,2048]{2,1,0:T(8,128)(2,1)}, u32[]{:S(2)}, u32[]{:S(2)}) %all-to-all-start.6) | async-done | bytes 6291488 | tf_op jit(solution)/shard_map/all_to_all | solution.py:66
  602.7 12.5 %gather_fusion.2 = bf16[1024,2048]{1,0:T(8,128)(2,1)} fusion(bf16[1536,2048]{1,0:T(8,128)(2,1)} %bitcast.28, s32[1024]{0:T(1024)S(1)} %broadcast_clamp_fusion), kind=kCustom, calls=%fused_computation.2 | custom fusion | bytes 8392704 | tf_op jit(solution)/shard_map/gather | solution.py:68
  615.2 5.7 fusion.1
  620.9 1.1 copy.82
  622.0 0.0 copy-done.1
  (16 shorter events, 0.1 us)
Async XLA Ops:
  7.2 222.1 %copy-start = (bf16[128,2048]{1,0:T(8,128)(2,1)S(1)}, bf16[128,2048]{1,0:T(8,128)(2,1)}, u32[]{:S(2)}) copy-start(bf16[128,2048]{1,0:T(8,128)(2,1)} %param.6) | copy-start | bytes 1572868
  7.2 19.3 %copy-start.3 = (bf16[1,192,2048]{2,1,0:T(8,128)(2,1)S(1)}, bf16[1,192,2048]{2,1,0:T(8,128)(2,1)}, u32[]{:S(2)}) copy-start(bf16[1,192,2048]{2,1,0:T(8,128)(2,1)} %param.11) | copy-start | bytes 2359300
  13.3 64.4 %all-to-all-start.1 = ((bf16[1,2,192,2048]{2,1,0,3:T(2,128)(2,1)}), bf16[1,2,192,2048]{2,1,0,3:T(2,128)(2,1)S(1)}, u32[]{:S(2)}, u32[]{:S(2)}) async-start(bf16[1,2,192,2048]{2,1,0,3:T(2,128)(2,1)} %copy.60), calls=%async_computation.1 | async-start | bytes 4194304 | tf_op jit(solution)/shard_map/all_to_all | solution.py:31
  26.5 57.1 %copy-start.6 = (s32[64]{0:T(128)S(1)}, s32[64]{0:T(128)}, u32[]{:S(2)}) copy-start(s32[64]{0:T(128)} %param.9) | copy-start | bytes 772
  77.8 6.0 copy-start.2
  77.8 28.8 %all-to-all-start.4 = ((bf16[64,2,3072]{2,1,0:T(2,128)(2,1)}), bf16[64,2,3072]{2,1,0:T(2,128)(2,1)S(1)}, u32[]{:S(2)}, u32[]{:S(2)}) async-start(bf16[64,2,3072]{2,1,0:T(2,128)(2,1)} %reshape.169), calls=%async_computation.4 | async-start | bytes 1572864 | tf_op jit(solution)/shard_map/all_to_all | solution.py:32
  106.6 57.6 %all-to-all-start.2 = ((bf16[64,2,192,32]{2,3,1,0:T(8,128)(2,1)}), bf16[64,2,192,32]{2,3,1,0:T(8,128)(2,1)}, u32[]{:S(2)}, u32[]{:S(2)}) async-start(bf16[64,2,192,32]{2,3,1,0:T(8,128)(2,1)} %broadcast_select_fusion), calls=%async_computation.2 | async-start | bytes 4194304 | tf_op jit(solution)/shard_map/all_to_all | solution.py:36
  164.1 34.5 %all-to-all-start.5 = ((bf16[64,1,192,32]{2,3,1,0:T(8,128)(2,1)}), bf16[64,1,192,32]{2,3,1,0:T(8,128)(2,1)}, u32[]{:S(2)}, u32[]{:S(2)}) async-start(bf16[64,1,192,32]{2,3,1,0:T(8,128)(2,1)} %fusion.10), calls=%async_computation.5 | async-start | bytes 2097152 | tf_op jit(solution)/shard_map/all_to_all | solution.py:37
  204.5 5.6 copy-start.4
  204.5 76.8 %all-to-all-start.3 = ((bf16[1,2,768,2048]{3,1,0,2:T(2,128)(2,1)}), bf16[1,2,768,2048]{3,1,0,2:T(2,128)(2,1)}, u32[]{:S(2)}, u32[]{:S(2)}) async-start(bf16[1,2,768,2048]{3,1,0,2:T(2,128)(2,1)} %bitcast.81), calls=%async_computation.3 | async-start | bytes 12582912 | tf_op jit(solution)/shard_map/all_to_all | solution.py:10
  281.3 147.5 %all-to-all-start = ((bf16[64,24,2048]{2,1,0:T(8,128)(2,1)}), bf16[64,24,2048]{2,1,0:T(8,128)(2,1)}, u32[]{:S(2)}, u32[]{:S(2)}) async-start(bf16[64,24,2048]{2,1,0:T(8,128)(2,1)} %bitcast.80), calls=%async_computation | async-start | bytes 12582912 | tf_op jit(solution)/shard_map/all_to_all | solution.py:56
  288.0 156.4 %all-gather.2.cloned.1.call-start = ((), (), s32[]{:S(2)}) async-start(), calls=%async_computation.7 | async-start | bytes 3932160 | tf_op jit(solution)/shard_map/all_gather | solution.py:43
  455.8 6.1 copy-start.5
  455.8 146.9 %all-to-all-start.6 = ((bf16[64,24,2048]{2,1,0:T(8,128)(2,1)}), bf16[64,24,2048]{2,1,0:T(8,128)(2,1)}, u32[]{:S(2)}, u32[]{:S(2)}) async-start(bf16[64,24,2048]{2,1,0:T(8,128)(2,1)} %bitcast.88), calls=%async_computation.6 | async-start | bytes 12582912 | tf_op jit(solution)/shard_map/all_to_all | solution.py:66
  602.7 19.3 %copy-start.1 = (bf16[128,2048]{1,0:T(8,128)(2,1)S(1)}, bf16[128,2048]{1,0:T(8,128)(2,1)}, u32[]{:S(2)}) copy-start(bf16[128,2048]{1,0:T(8,128)(2,1)} %param.6) | copy-start | bytes 1572868
Sparse Core Ops, SparseCore 0:
  291.2 41.1 all-gather.1
